TPU v7x, 256 devices: a whole 4x4x8 slice. The times are simulated.
256 devices in a mesh: view: 16 (over z, y_hi), row: 16 (over x, y_lo, core).
Axes of the slice: x: 4, y: 4 (y_hi: 2, y_lo: 2; y = y_hi * 2 + y_lo), z: 8, core: 2. Of those that a mesh axis runs over, the one named last changes fastest.
Arguments:
- latent: bfloat16 [1, 16, 32, 72, 1280], P(None, 'view', 'row'), may hold values from -30 to 30
- gn_gain: float32 [1280], replicated, may hold values from 0.25 to 1.75
- gn_bias: float32 [1280], replicated, may hold values from -3 to 3
- cam_idx: int32 [1, 16], P(None, 'view'), may hold values from 0 to 63
- noise_idx: int32 [1], replicated, may hold values from 0 to 999
- cam_table: bfloat16 [64, 2560], replicated, may hold values from -2 to 2
- noise_table: bfloat16 [1000, 2560], replicated, may hold values from -2 to 2
- conv_w: bfloat16 [3, 3, 1280, 1280], P(None, None, None, 'row'), may hold values from -0.0546875 to 0.0546875
- conv_bias: float32 [1280], replicated, may hold values from -3 to 3
- ln_gain: float32 [1280], replicated, may hold values from 0.25 to 1.75
- attn_in: bfloat16 [3, 1280, 1280], P(None, None, 'view'), may hold values from -0.15625 to 0.15625
- attn_out: bfloat16 [1280, 1280], P('view'), may hold values from -0.15625 to 0.15625
- head_scale: float32 [20], replicated, may hold values from 0.4 to 135
Outputs:
- block_out: bfloat16 [1, 16, 32, 72, 1280], P(None, 'view', 'row')
All inputs are finite; a program needn't handle non-finite values.
Results may differ from a plain program's by a relative error of at most 0.02.
Values may be sent and summed in bfloat16 or wider, within the bound.
No kernel may reach another device: no remote copies, remote signals or barrier semaphores. Data moves between devices by JAX's collectives and lax.ppermute only.
A program may use at most 192 MiB of HBM per device.

v0:
```python
import math
import jax
import jax.numpy as jnp
from jax import lax
from jax.sharding import PartitionSpec as P

GROUPS = 32
epsilon = 1e-05


def convolve(padded, weight, out_rows, out_cols):
    channels = padded.shape[-1]
    summed = jnp.zeros(
        (padded.shape[0] * padded.shape[1] * out_rows * out_cols, weight.shape[-1]), jnp.float32
    )
    for tap_row in range(3):
        for tap_col in range(3):
            tap_rows = padded[
                :, :, tap_row : tap_row + out_rows, tap_col : tap_col + out_cols, :
            ].reshape(-1, channels)
            summed = summed + jnp.dot(
                tap_rows, weight[tap_row, tap_col], preferred_element_type=jnp.float32
            )
    return summed.reshape(padded.shape[0], padded.shape[1], out_rows, out_cols, weight.shape[-1])


def attend(query, key_block, value, head_scale):
    view_count = query.shape[0]
    item_count = query.shape[2]
    channels = query.shape[3]
    head_count = head_scale.shape[0]
    head_size = channels // head_count
    query_heads = query.reshape(view_count, item_count, head_count, head_size)
    key_heads = key_block.reshape(view_count, item_count, head_count, head_size)
    value_heads = value.reshape(view_count, item_count, head_count, head_size)
    scores = jnp.einsum(
        "vihd,uihd->ihvu", query_heads, key_heads, preferred_element_type=jnp.float32
    )
    scores = scores * (head_scale / math.sqrt(head_size))[None, :, None, None]
    peak_score = jnp.max(scores, axis=-1, keepdims=True)
    exp_scores = jnp.exp(scores - peak_score)
    soft_weights = (exp_scores / jnp.sum(exp_scores, axis=-1, keepdims=True)).astype(jnp.bfloat16)
    mixed = jnp.einsum(
        "ihvu,uihd->vihd", soft_weights, value_heads, preferred_element_type=jnp.float32
    )
    return mixed.astype(jnp.bfloat16).reshape(view_count, 1, item_count, channels)


def send_back(mixed):
    return lax.all_to_all(mixed, "view", split_axis=0, concat_axis=1, tiled=True)


def local(
    latent,
    gn_gain,
    gn_bias,
    cam_idx,
    noise_idx,
    cam_table,
    noise_table,
    conv_w,
    conv_bias,
    ln_gain,
    attn_in,
    attn_out,
    head_scale,
):
    samples, local_views, local_rows, local_cols, channels = latent.shape
    width_out = ln_gain.shape[0]
    x_float = latent.astype(jnp.float32)
    grouped = x_float.reshape(
        samples, local_views, local_rows, local_cols, GROUPS, channels // GROUPS
    )
    entries = local_rows * local_cols * (channels // GROUPS) * lax.axis_size("row")
    summed = lax.psum(jnp.sum(grouped, axis=(2, 3, 5)), "row")
    average = (summed / entries)[:, :, None, None, :, None]
    centred = grouped - average
    spread = lax.psum(jnp.sum(centred * centred, axis=(2, 3, 5)), "row")
    variance = (spread / entries)[:, :, None, None, :, None]
    normed = (centred * lax.rsqrt(variance + epsilon)).reshape(x_float.shape)
    cam_hot = (cam_idx[:, :, None] == jnp.arange(cam_table.shape[0], dtype=jnp.int32)).astype(
        jnp.bfloat16
    )
    cam_film = jnp.einsum("svn,nc->svc", cam_hot, cam_table, preferred_element_type=jnp.float32)
    noise_hot = (noise_idx[:, None] == jnp.arange(noise_table.shape[0], dtype=jnp.int32)).astype(
        jnp.bfloat16
    )
    noise_film = jnp.dot(noise_hot, noise_table, preferred_element_type=jnp.float32)
    film_rows = cam_film + noise_film[:, None, :]
    film_scale = film_rows[:, :, None, None, :channels]
    film_shift = film_rows[:, :, None, None, channels:]
    hidden = (normed * gn_gain + gn_bias) * (1.0 + film_scale) + film_shift
    activated = jax.nn.silu(hidden).astype(jnp.bfloat16)
    all_rows_act = lax.all_gather(activated, "row", axis=2, tiled=True)
    padded = jnp.pad(all_rows_act, ((0, 0), (0, 0), (1, 1), (1, 1), (0, 0)))
    partial_out = convolve(padded, conv_w, all_rows_act.shape[2], local_cols)
    conv_out = lax.all_to_all(partial_out, "row", split_axis=2, concat_axis=4, tiled=True)
    resid_out = (x_float + conv_out + conv_bias).astype(jnp.bfloat16)
    resid_float = resid_out.astype(jnp.float32)
    middle = jnp.mean(resid_float, axis=-1, keepdims=True)
    spread_y = jnp.mean((resid_float - middle) ** 2, axis=-1, keepdims=True)
    normed_y = ((resid_float - middle) * lax.rsqrt(spread_y + epsilon) * ln_gain).astype(
        jnp.bfloat16
    )
    weights_in = lax.all_gather(attn_in, "view", axis=2, tiled=True)
    view_devices = lax.axis_size("view")
    per_device = samples * local_rows * local_cols // view_devices
    pixel_major = jnp.moveaxis(normed_y, 1, 0).reshape(
        local_views, view_devices, per_device, width_out
    )

    def project(pixel_block, matrix_index):
        block_shape = pixel_block.shape
        flat_block = pixel_block.reshape(-1, width_out)
        return (
            jnp.dot(flat_block, weights_in[matrix_index], preferred_element_type=jnp.float32)
            .astype(jnp.bfloat16)
            .reshape(block_shape)
        )

    triple_in = (project(pixel_major, 0), project(pixel_major, 1), project(pixel_major, 2))
    mixed = send_back(
        attend(
            lax.all_to_all(triple_in[0], "view", split_axis=1, concat_axis=0, tiled=True),
            lax.all_to_all(triple_in[1], "view", split_axis=1, concat_axis=0, tiled=True),
            lax.all_to_all(triple_in[2], "view", split_axis=1, concat_axis=0, tiled=True),
            head_scale,
        )
    )
    mixed = jnp.moveaxis(
        mixed.reshape(local_views, samples, local_rows, local_cols, width_out), 0, 1
    )
    flat_mixed = mixed.reshape(-1, width_out)
    projected = jnp.dot(
        flat_mixed,
        lax.all_gather(attn_out, "view", axis=0, tiled=True),
        preferred_element_type=jnp.float32,
    )
    return (resid_float + projected.reshape(resid_float.shape)).astype(jnp.bfloat16)


def solution(mesh):
    placed = (
        P(None, "view", "row", None, None),
        P(),
        P(),
        P(None, "view"),
        P(),
        P(),
        P(),
        P(None, None, None, "row"),
        P(),
        P(),
        P(None, None, "view"),
        P("view", None),
        P(),
    )
    return jax.shard_map(
        local,
        mesh=mesh,
        in_specs=placed,
        out_specs=P(None, "view", "row", None, None),
        check_vma=False,
    )
```

profile of v0, /device:TPU:2, one launch (start us, length us, event | category | flops | bytes accessed | tf_op | source)
XLA Modules:
  0.0 409.6 jit_solution(9763920457493276366)
XLA Ops:
  6.6 1.1 convert_reduce_fusion.1
  7.9 23.6 %psum.14 = f32[1,1,32]{2,1,0:T(1,128)S(1)} all-reduce(f32[1,1,32]{2,1,0:T(1,128)S(1)} %bitcast.140), channel_id=1, replica_groups=mesh['view'=16,'row'=16] {'row'}, use_global_device_ids=true, to_apply=%region_2.0 | all-reduce | flops 32 | bytes 256 | tf_op jit(solution)/shard_map/psum | solution.py:75
  31.7 1.1 fusion.28
  33.0 27.1 %psum.15 = f32[1,1,32]{2,1,0:T(1,128)S(1)} all-reduce(f32[1,1,32]{2,1,0:T(1,128)S(1)} %bitcast.139), channel_id=1, replica_groups=mesh['view'=16,'row'=16] {'row'}, use_global_device_ids=true, to_apply=%region_5.6 | all-reduce | flops 32 | bytes 256 | tf_op jit(solution)/shard_map/psum | solution.py:78
  61.6 3.2 convolution_reduce_fusion
  67.7 48.7 %all-gather.4.cloned.1.call-done = bf16[1,1,32,72,1280]{4,3,1,0,2:T(8,128)(2,1)} async-done(((bf16[1,1,2,72,1280]{4,3,1,0,2:T(8,128)(2,1)}), bf16[1,1,32,72,1280]{4,3,1,0,2:T(8,128)(2,1)}) %all-gather.4.cloned.1.call-update) | async-done | bytes 5898256 | tf_op jit(solution)/shard_map/all_gather | solution.py:94
  116.4 35.4 %pad_slice_fusion = (bf16[1,1,32,72,1280]{4,3,1,0,2:T(8,128)(2,1)S(1)}, bf16[1,1,32,72,1280]{4,3,1,0,2:T(8,128)(2,1)}, bf16[1,1,32,72,1280]{4,3,1,0,2:T(8,128)(2...) fusion(bf16[1,1,32,72,1280]{4,3,1,0,2:T(8,128)(2,1)} %all-gathe, ...), kind=kLoop, calls=%fused_computation.1 | loop fusion | bytes 53084160 | tf_op jit(solution)/shard_map/slice | solution.py:18
  151.9 4.8 %fusion.48 = f32[2304,80]{0,1:T(8,128)S(1)} fusion(bf16[2304,1280]{1,0:T(8,128)(2,1)} %bitcast.132, bf16[3,3,1280,80]{2,3,1,0:T(8,128)(2,1)S(1)} %copy-done.4), kind=kOutput, calls=%fused_computation.73 | convolution fusion | flops 471859200 | bytes 6840320 | tf_op jit(solution)/shard_map/dot_general | solution.py:21
  156.7 4.8 %convolution_add_fusion.7 = f32[2304,80]{0,1:T(8,128)S(1)} fusion(f32[2304,80]{0,1:T(8,128)S(1)} %fusion.48, bf16[2304,1280]{1,0:T(8,128)(2,1)} %bitcast.131, bf16[3,3,1280,80]{2,3,1,0:T(8,128)(2,1)S(1)} %copy-done.4), kind=kOutput, calls=%fused_computation.16 | convolution fusion | flops 472043520 | bytes 7577600 | tf_op jit(solution)/shard_map/dot_general | solution.py:21
  161.5 1.9 convolution_add_fusion.6
  163.5 1.9 convolution_add_fusion.5
  165.7 1.9 convolution_add_fusion.4
  167.6 1.9 convolution_add_fusion.3
  169.8 1.9 convolution_add_fusion.2
  171.7 1.9 convolution_add_fusion.1
  173.7 2.9 convolution_add_fusion
  176.9 23.6 %all_to_all.54 = f32[1,1,32,72,80]{4,3,1,0,2:T(8,128)S(1)} all-to-all(f32[1,1,32,72,80]{4,3,1,0,2:T(8,128)S(1)} %bitcast.134), channel_id=1, replica_groups=mesh['view'=16,'row'=16] {'row'}, dimensions={2} | all-to-all | bytes 1474560 | tf_op jit(solution)/shard_map/all_to_all | solution.py:97
  202.2 80.4 %all-gather.6.cloned.1.call-done = bf16[3,1280,1280]{1,2,0:T(8,128)(2,1)} async-done(((bf16[3,1280,80]{1,2,0:T(8,128)(2,1)}), bf16[3,1280,1280]{1,2,0:T(8,128)(2,1)}) %all-gather.6.cloned.1.call-update) | async-done | bytes 9830416 | tf_op jit(solution)/shard_map/all_gather | solution.py:105
  282.6 3.2 fusion.16
  286.8 4.4 %all-to-all-start.2 = ((bf16[1,16,9,1280]{3,2,0,1:T(8,128)(2,1)}), bf16[1,16,9,1280]{3,2,0,1:T(8,128)(2,1)S(1)}, u32[]{:S(2)}, u32[]{:S(2)}) async-start(bf16[1,16,9,1280]{3,2,0,1:T(8,128)(2,1)} %bitcast.33), calls=%async_computation.2 | async-start | bytes 1310720 | tf_op jit(solution)/shard_map/all_to_all | solution.py:124
  291.3 3.2 fusion.17
  295.4 20.7 %all-to-all-done.2 = bf16[1,16,9,1280]{3,2,0,1:T(8,128)(2,1)S(1)} async-done(((bf16[1,16,9,1280]{3,2,0,1:T(8,128)(2,1)}), bf16[1,16,9,1280]{3,2,0,1:T(8,128)(2,1)S(1)}, u32[]{:S(2)}, u32[]{:S(2)}) %all-to-all-start.2) | async-done | bytes 368672 | tf_op jit(solution)/shard_map/all_to_all | solution.py:124
  316.1 3.8 all-to-all-start.3
  319.9 3.2 fusion.15
  324.1 16.3 %all-to-all-done.3 = bf16[1,16,9,1280]{3,2,0,1:T(8,128)(2,1)S(1)} async-done(((bf16[1,16,9,1280]{3,2,0,1:T(8,128)(2,1)}), bf16[1,16,9,1280]{3,2,0,1:T(8,128)(2,1)S(1)}, u32[]{:S(2)}, u32[]{:S(2)}) %all-to-all-start.3) | async-done | bytes 368672 | tf_op jit(solution)/shard_map/all_to_all | solution.py:125
  340.4 3.6 all-to-all-start.1
  344.6 1.6 reshape.215
  346.2 19.4 %all-to-all-done.1 = bf16[1,16,9,1280]{3,2,0,1:T(8,128)(2,1)S(1)} async-done(((bf16[1,16,9,1280]{3,2,0,1:T(8,128)(2,1)}), bf16[1,16,9,1280]{3,2,0,1:T(8,128)(2,1)S(1)}, u32[]{:S(2)}, u32[]{:S(2)}) %all-to-all-start.1) | async-done | bytes 368672 | tf_op jit(solution)/shard_map/all_to_all | solution.py:126
  366.2 3.2 fusion.69
  369.4 1.9 fusion.20
  372.1 27.4 %all_to_all.55 = bf16[16,1,9,1280]{3,2,1,0:T(8,128)(2,1)S(1)} all-to-all(bf16[16,1,9,1280]{3,2,1,0:T(8,128)(2,1)S(1)} %reshape.216), channel_id=1, replica_groups=mesh['view'=16,'row'=16] {'view'}, dimensions={0} | all-to-all | bytes 737280 | tf_op jit(solution)/shard_map/all_to_all | solution.py:50
  399.7 3.3 fusion.12
  (81 shorter events, 11.4 us)
Async XLA Ops:
  6.5 58.3 %copy-start = (bf16[64,2560]{1,0:T(8,128)(2,1)S(1)}, bf16[64,2560]{1,0:T(8,128)(2,1)}, u32[]{:S(2)}) copy-start(bf16[64,2560]{1,0:T(8,128)(2,1)} %param.18) | copy-start | bytes 983044
  6.5 58.6 %copy-start.3 = (bf16[1,1,2,72,1280]{4,3,2,1,0:T(8,128)(2,1)S(1)}, bf16[1,1,2,72,1280]{4,3,2,1,0:T(8,128)(2,1)}, u32[]{:S(2)}) copy-start(bf16[1,1,2,72,1280]{4,3,2,1,0:T(8,128)(2,1)} %param.13) | copy-start | bytes 1105924
  6.5 58.6 %copy-start.6 = (f32[1280]{0:T(1024)S(1)}, f32[1280]{0:T(1024)}, u32[]{:S(2)}) copy-start(f32[1280]{0:T(1024)} %param.14) | copy-start | bytes 15364
  6.5 58.6 %copy-start.5 = (f32[1280]{0:T(1024)S(1)}, f32[1280]{0:T(1024)}, u32[]{:S(2)}) copy-start(f32[1280]{0:T(1024)} %param.15) | copy-start | bytes 15364
  6.5 109.9 %all-gather.4.cloned.1.call-start = ((), (), s32[]{:S(2)}) async-start(), calls=%async_computation.5 | async-start | bytes 6266880 | tf_op jit(solution)/shard_map/all_gather | solution.py:94
  66.2 216.4 %all-gather.6.cloned.1.call-start = ((), (), s32[]{:S(2)}) async-start(), calls=%async_computation.6 | async-start | bytes 10444800 | tf_op jit(solution)/shard_map/all_gather | solution.py:105
  67.0 332.7 %all-gather.8.cloned.1.call-start = ((), (), s32[]{:S(2)}) async-start(), calls=%async_computation.7 | async-start | bytes 3481600 | tf_op jit(solution)/shard_map/all_gather | solution.py:136
  67.7 84.1 %copy-start.4 = (bf16[3,3,1280,80]{2,3,1,0:T(8,128)(2,1)S(1)}, bf16[3,3,1280,80]{2,3,1,0:T(8,128)(2,1)}, u32[]{:S(2)}) copy-start(bf16[3,3,1280,80]{2,3,1,0:T(8,128)(2,1)} %param.20) | copy-start | bytes 5529604
  151.9 11.6 %slice-start.6 = ((s8[5898240]{0:T(1024)(128)(4,1)}), s8[4194304]{0:T(1024)(128)(4,1)S(1)}, s32[]{:S(2)}) async-start(s8[5898240]{0:T(1024)(128)(4,1)} %bitcast.127), calls=%async_computation.14 | async-start | bytes 8388608
  156.6 4.8 %copy-start.2 = (bf16[1,1,32,72,1280]{4,3,1,0,2:T(8,128)(2,1)S(1)}, bf16[1,1,32,72,1280]{4,3,1,0,2:T(8,128)(2,1)}, u32[]{:S(2)}) copy-start(bf16[1,1,32,72,1280]{4,3,1,0,2:T(8,128)(2,1)} %get-tuple-element.11) | copy-start | bytes 17694724
  156.7 6.8 %slice-start.7 = ((s8[5898240]{0:T(1024)(128)(4,1)}), s8[1703936]{0:T(1024)(128)(4,1)S(1)}, s32[]{:S(2)}) async-start(s8[5898240]{0:T(1024)(128)(4,1)} %bitcast.127), calls=%async_computation.15 | async-start | bytes 3407872
  161.5 3.9 slice-start
  161.5 6.1 %slice-start.4 = ((s8[5898240]{0:T(1024)(128)(4,1)}), s8[4194304]{0:T(1024)(128)(4,1)S(1)}, s32[]{:S(2)}) async-start(s8[5898240]{0:T(1024)(128)(4,1)} %bitcast.124), calls=%async_computation.12 | async-start | bytes 8388608
  163.4 2.2 slice-start.1
  163.5 4.2 %slice-start.5 = ((s8[5898240]{0:T(1024)(128)(4,1)}), s8[1703936]{0:T(1024)(128)(4,1)S(1)}, s32[]{:S(2)}) async-start(s8[5898240]{0:T(1024)(128)(4,1)} %bitcast.124), calls=%async_computation.13 | async-start | bytes 3407872
  165.7 3.9 slice-start.2
  167.6 2.2 slice-start.3
  176.5 24.9 %copy-start.7 = (f32[1280]{0:T(1024)S(1)}, f32[1280]{0:T(1024)}, u32[]{:S(2)}) copy-start(f32[1280]{0:T(1024)} %param.21) | copy-start | bytes 15364
  176.6 25.4 %copy-start.8 = (f32[1280]{0:T(1024)S(1)}, f32[1280]{0:T(1024)}, u32[]{:S(2)}) copy-start(f32[1280]{0:T(1024)} %param.22) | copy-start | bytes 15364
  286.8 29.3 %all-to-all-start.2 = ((bf16[1,16,9,1280]{3,2,0,1:T(8,128)(2,1)}), bf16[1,16,9,1280]{3,2,0,1:T(8,128)(2,1)S(1)}, u32[]{:S(2)}, u32[]{:S(2)}) async-start(bf16[1,16,9,1280]{3,2,0,1:T(8,128)(2,1)} %bitcast.33), calls=%async_computation.2 | async-start | bytes 1310720 | tf_op jit(solution)/shard_map/all_to_all | solution.py:124
  294.4 49.6 %copy-start.9 = (f32[20]{0:T(128)S(1)}, f32[20]{0:T(128)}, u32[]{:S(2)}) copy-start(f32[20]{0:T(128)} %param.25) | copy-start | bytes 244
  316.1 24.2 %all-to-all-start.3 = ((bf16[1,16,9,1280]{3,2,0,1:T(8,128)(2,1)}), bf16[1,16,9,1280]{3,2,0,1:T(8,128)(2,1)S(1)}, u32[]{:S(2)}, u32[]{:S(2)}) async-start(bf16[1,16,9,1280]{3,2,0,1:T(8,128)(2,1)} %bitcast.35), calls=%async_computation.3 | async-start | bytes 1310720 | tf_op jit(solution)/shard_map/all_to_all | solution.py:125
  340.4 25.2 %all-to-all-start.1 = ((bf16[1,16,9,1280]{3,2,0,1:T(8,128)(2,1)}), bf16[1,16,9,1280]{3,2,0,1:T(8,128)(2,1)S(1)}, u32[]{:S(2)}, u32[]{:S(2)}) async-start(bf16[1,16,9,1280]{3,2,0,1:T(8,128)(2,1)} %bitcast.31), calls=%async_computation.1 | async-start | bytes 1310720 | tf_op jit(solution)/shard_map/all_to_all | solution.py:126
  369.4 33.6 %copy-start.1 = (bf16[64,2560]{1,0:T(8,128)(2,1)S(1)}, bf16[64,2560]{1,0:T(8,128)(2,1)}, u32[]{:S(2)}) copy-start(bf16[64,2560]{1,0:T(8,128)(2,1)} %param.18) | copy-start | bytes 983044
Sparse Core Ops, SparseCore 0:
  66.3 50.0 all-gather.3
  119.0 163.5 all-gather.5
  285.2 112.3 all-gather.7
where the time goes:
time: 410 us
  waiting for transfers between devices  187 us (46%)
  blocking collectives  102 us (25%)
  matrix products  45.2 us (11%)
  local copies, waits for them, and re-layouts  44.6 us (11%)
  between operations  14.9 us (4%)
  starting transfers between devices  12 us (3%)
  other arithmetic  4.32 us (1%)
    all_gather x1, waiting for transfers between devices, local(): weights_in = lax.all_gather(attn_in, 'view', axis=2, tiled=True)  80.4 us
    all_gather x1, waiting for transfers between devices, local(): all_rows_act = lax.all_gather(activated, 'row', axis=2, tiled=True)  48.7 us
    slice x1, local copies, waits for them, and re-layouts, convolve(): padded[:, :, tap_row:tap_row + out_rows, tap_col:tap_col + out_cols, :]  35.4 us
    all_to_all x1, blocking collectives, send_back(): lax.all_to_all(mixed, 'view', split_axis=0, concat_axis=1, tiled=True)  27.4 us
    psum x1, blocking collectives, local(): spread = lax.psum(jnp.sum(centred * centred, axis=(2, 3, 5)), 'row')  27.1 us
    dot_general x9, matrix products, convolve(): jnp.dot(tap_rows, weight[tap_row, tap_col], preferred_element_type=jnp.fl...  23.9 us
    psum x1, blocking collectives, local(): summed = lax.psum(jnp.sum(grouped, axis=(2, 3, 5)), 'row')  23.6 us
    all_to_all x1, blocking collectives, local(): lax.all_to_all(partial_out, 'row', split_axis=2, concat_axis=4, tiled=True)  23.6 us
  transfers between devices with their start and end apart: 6, of which 5 were waited for; matrix products, arithmetic and copies ran while one was open for 20% of the time, Pallas kernels for 0%

commit v1 on v0

--- a/solution.py
+++ b/solution.py
@@ -72,7 +72,7 @@
         samples, local_views, local_rows, local_cols, GROUPS, channels // GROUPS
     )
     entries = local_rows * local_cols * (channels // GROUPS) * lax.axis_size("row")
-    summed = lax.psum(jnp.sum(grouped, axis=(2, 3, 5)), "row")
+    summed = jnp.sum(lax.all_gather(jnp.sum(grouped, axis=(2, 3, 5)), "row"), axis=0)
     average = (summed / entries)[:, :, None, None, :, None]
     centred = grouped - average
     spread = lax.psum(jnp.sum(centred * centred, axis=(2, 3, 5)), "row")

time: 410 us -> 413 us (level)
    psum x1 -> x0, blocking collectives: 23.6 us -> none  [local(): summed = lax.psum(jnp.sum(grouped, axis=(2, 3, 5)), 'row')]
    unnamed x0 -> x1, blocking collectives: none -> 23.6 us
where the time goes in v1:
time: 413 us; the launch traced here: 412 us
  waiting for transfers between devices  186 us (45%)
  blocking collectives  101 us (24%)
  local copies, waits for them, and re-layouts  47.3 us (11%)
  matrix products  45.5 us (11%)
  between operations  15.6 us (4%)
  starting transfers between devices  12 us (3%)
  other arithmetic  4.34 us (1%)
    all_gather x1, waiting for transfers between devices, local(): weights_in = lax.all_gather(attn_in, 'view', axis=2, tiled=True)  80.2 us
    all_gather x1, waiting for transfers between devices, local(): all_rows_act = lax.all_gather(activated, 'row', axis=2, tiled=True)  48.7 us
    slice x1, local copies, waits for them, and re-layouts, convolve(): padded[:, :, tap_row:tap_row + out_rows, tap_col:tap_col + out_cols, :]  35.6 us
    psum x1, blocking collectives, local(): spread = lax.psum(jnp.sum(centred * centred, axis=(2, 3, 5)), 'row')  27.1 us
    all_to_all x1, blocking collectives, send_back(): lax.all_to_all(mixed, 'view', split_axis=0, concat_axis=1, tiled=True)  26.5 us
    dot_general x9, matrix products, convolve(): jnp.dot(tap_rows, weight[tap_row, tap_col], preferred_element_type=jnp.fl...  23.9 us
    all_to_all x1, blocking collectives, local(): lax.all_to_all(partial_out, 'row', split_axis=2, concat_axis=4, tiled=True)  23.7 us
    unnamed x1, blocking collectives  23.6 us
  transfers between devices with their start and end apart: 6, of which 5 were waited for; matrix products, arithmetic and copies ran while one was open for 20% of the time, Pallas kernels for 0%

profile of v1, /device:TPU:2, one launch (start us, length us, event | category | flops | bytes accessed | tf_op | source)
XLA Modules:
  0.0 411.9 jit_solution(17468110595046658931)
XLA Ops:
  7.9 1.3 dynamic-slice
  10.1 23.6 %all-reduce.1 = f32[512]{0:T(512)S(1)} all-reduce(f32[512]{0:T(512)S(1)} %dynamic-update-slice), channel_id=2, replica_groups=mesh['view'=16,'row'=16] {'row'}, use_global_device_ids=true, to_apply=%add.1 | all-reduce | flops 512 | bytes 4096
  35.2 27.1 %psum.7 = f32[1,1,32]{2,1,0:T(1,128)S(1)} all-reduce(f32[1,1,32]{2,1,0:T(1,128)S(1)} %bitcast.137), channel_id=1, replica_groups=mesh['view'=16,'row'=16] {'row'}, use_global_device_ids=true, to_apply=%region_5.6 | all-reduce | flops 32 | bytes 256 | tf_op jit(solution)/shard_map/psum | solution.py:78
  63.9 3.2 convolution_reduce_fusion
  70.0 48.7 %all-gather.5.cloned.1.call-done = bf16[1,1,32,72,1280]{4,3,1,0,2:T(8,128)(2,1)} async-done(((bf16[1,1,2,72,1280]{4,3,1,0,2:T(8,128)(2,1)}), bf16[1,1,32,72,1280]{4,3,1,0,2:T(8,128)(2,1)}) %all-gather.5.cloned.1.call-update) | async-done | bytes 5898256 | tf_op jit(solution)/shard_map/all_gather | solution.py:94
  118.7 35.6 %pad_slice_fusion = (bf16[1,1,32,72,1280]{4,3,1,0,2:T(8,128)(2,1)S(1)}, bf16[1,1,32,72,1280]{4,3,1,0,2:T(8,128)(2,1)}, bf16[1,1,32,72,1280]{4,3,1,0,2:T(8,128)(2...) fusion(bf16[1,1,32,72,1280]{4,3,1,0,2:T(8,128)(2,1)} %all-gathe, ...), kind=kLoop, calls=%fused_computation.1 | loop fusion | bytes 53084160 | tf_op jit(solution)/shard_map/slice | solution.py:18
  154.3 4.8 %fusion.48 = f32[2304,80]{0,1:T(8,128)S(1)} fusion(bf16[2304,1280]{1,0:T(8,128)(2,1)} %bitcast.130, bf16[3,3,1280,80]{2,3,1,0:T(8,128)(2,1)S(1)} %copy-done.4), kind=kOutput, calls=%fused_computation.73 | convolution fusion | flops 471859200 | bytes 6840320 | tf_op jit(solution)/shard_map/dot_general | solution.py:21
  159.1 4.8 %convolution_add_fusion.7 = f32[2304,80]{0,1:T(8,128)S(1)} fusion(f32[2304,80]{0,1:T(8,128)S(1)} %fusion.48, bf16[2304,1280]{1,0:T(8,128)(2,1)} %bitcast.129, bf16[3,3,1280,80]{2,3,1,0:T(8,128)(2,1)S(1)} %copy-done.4), kind=kOutput, calls=%fused_computation.16 | convolution fusion | flops 472043520 | bytes 7577600 | tf_op jit(solution)/shard_map/dot_general | solution.py:21
  163.9 1.9 convolution_add_fusion.6
  165.9 1.9 convolution_add_fusion.5
  168.1 1.9 convolution_add_fusion.4
  170.1 1.9 convolution_add_fusion.3
  172.2 1.9 convolution_add_fusion.2
  174.2 1.9 convolution_add_fusion.1
  176.1 2.9 convolution_add_fusion
  179.4 23.7 %all_to_all.54 = f32[1,1,32,72,80]{4,3,1,0,2:T(8,128)S(1)} all-to-all(f32[1,1,32,72,80]{4,3,1,0,2:T(8,128)S(1)} %bitcast.132), channel_id=1, replica_groups=mesh['view'=16,'row'=16] {'row'}, dimensions={2} | all-to-all | bytes 1474560 | tf_op jit(solution)/shard_map/all_to_all | solution.py:97
  204.7 80.2 %all-gather.7.cloned.1.call-done = bf16[3,1280,1280]{1,2,0:T(8,128)(2,1)} async-done(((bf16[3,1280,80]{1,2,0:T(8,128)(2,1)}), bf16[3,1280,1280]{1,2,0:T(8,128)(2,1)}) %all-gather.7.cloned.1.call-update) | async-done | bytes 9830416 | tf_op jit(solution)/shard_map/all_gather | solution.py:105
  284.9 3.1 fusion.16
  289.1 4.5 %all-to-all-start.2 = ((bf16[1,16,9,1280]{3,2,0,1:T(8,128)(2,1)}), bf16[1,16,9,1280]{3,2,0,1:T(8,128)(2,1)S(1)}, u32[]{:S(2)}, u32[]{:S(2)}) async-start(bf16[1,16,9,1280]{3,2,0,1:T(8,128)(2,1)} %bitcast.32), calls=%async_computation.2 | async-start | bytes 1310720 | tf_op jit(solution)/shard_map/all_to_all | solution.py:124
  293.6 3.2 fusion.17
  297.7 20.9 %all-to-all-done.2 = bf16[1,16,9,1280]{3,2,0,1:T(8,128)(2,1)S(1)} async-done(((bf16[1,16,9,1280]{3,2,0,1:T(8,128)(2,1)}), bf16[1,16,9,1280]{3,2,0,1:T(8,128)(2,1)S(1)}, u32[]{:S(2)}, u32[]{:S(2)}) %all-to-all-start.2) | async-done | bytes 368672 | tf_op jit(solution)/shard_map/all_to_all | solution.py:124
  318.6 3.8 all-to-all-start.3
  322.5 3.2 fusion.15
  326.6 15.9 %all-to-all-done.3 = bf16[1,16,9,1280]{3,2,0,1:T(8,128)(2,1)S(1)} async-done(((bf16[1,16,9,1280]{3,2,0,1:T(8,128)(2,1)}), bf16[1,16,9,1280]{3,2,0,1:T(8,128)(2,1)S(1)}, u32[]{:S(2)}, u32[]{:S(2)}) %all-to-all-start.3) | async-done | bytes 368672 | tf_op jit(solution)/shard_map/all_to_all | solution.py:125
  342.5 3.6 all-to-all-start.1
  346.8 1.6 reshape.229
  348.4 19.2 %all-to-all-done.1 = bf16[1,16,9,1280]{3,2,0,1:T(8,128)(2,1)S(1)} async-done(((bf16[1,16,9,1280]{3,2,0,1:T(8,128)(2,1)}), bf16[1,16,9,1280]{3,2,0,1:T(8,128)(2,1)S(1)}, u32[]{:S(2)}, u32[]{:S(2)}) %all-to-all-start.1) | async-done | bytes 368672 | tf_op jit(solution)/shard_map/all_to_all | solution.py:126
  367.5 1.6 reshape.227
  369.1 3.2 fusion.69
  372.3 2.1 fusion.20
  375.3 26.5 %all_to_all.55 = bf16[16,1,9,1280]{3,2,1,0:T(8,128)(2,1)S(1)} all-to-all(bf16[16,1,9,1280]{3,2,1,0:T(8,128)(2,1)S(1)} %reshape.230), channel_id=1, replica_groups=mesh['view'=16,'row'=16] {'view'}, dimensions={0} | all-to-all | bytes 737280 | tf_op jit(solution)/shard_map/all_to_all | solution.py:50
  402.0 3.3 fusion.12
  (86 shorter events, 13.3 us)
Async XLA Ops:
  6.5 60.6 %copy-start = (bf16[64,2560]{1,0:T(8,128)(2,1)S(1)}, bf16[64,2560]{1,0:T(8,128)(2,1)}, u32[]{:S(2)}) copy-start(bf16[64,2560]{1,0:T(8,128)(2,1)} %param.18) | copy-start | bytes 983044
  6.5 60.8 %copy-start.3 = (bf16[1,1,2,72,1280]{4,3,2,1,0:T(8,128)(2,1)S(1)}, bf16[1,1,2,72,1280]{4,3,2,1,0:T(8,128)(2,1)}, u32[]{:S(2)}) copy-start(bf16[1,1,2,72,1280]{4,3,2,1,0:T(8,128)(2,1)} %param.13) | copy-start | bytes 1105924
  6.5 60.8 %copy-start.6 = (f32[1280]{0:T(1024)S(1)}, f32[1280]{0:T(1024)}, u32[]{:S(2)}) copy-start(f32[1280]{0:T(1024)} %param.14) | copy-start | bytes 15364
  6.5 60.9 %copy-start.5 = (f32[1280]{0:T(1024)S(1)}, f32[1280]{0:T(1024)}, u32[]{:S(2)}) copy-start(f32[1280]{0:T(1024)} %param.15) | copy-start | bytes 15364
  6.5 112.1 %all-gather.5.cloned.1.call-start = ((), (), s32[]{:S(2)}) async-start(), calls=%async_computation.5 | async-start | bytes 6266880 | tf_op jit(solution)/shard_map/all_gather | solution.py:94
  68.5 216.4 %all-gather.7.cloned.1.call-start = ((), (), s32[]{:S(2)}) async-start(), calls=%async_computation.6 | async-start | bytes 10444800 | tf_op jit(solution)/shard_map/all_gather | solution.py:105
  69.2 332.7 %all-gather.9.cloned.1.call-start = ((), (), s32[]{:S(2)}) async-start(), calls=%async_computation.7 | async-start | bytes 3481600 | tf_op jit(solution)/shard_map/all_gather | solution.py:136
  70.0 84.3 %copy-start.4 = (bf16[3,3,1280,80]{2,3,1,0:T(8,128)(2,1)S(1)}, bf16[3,3,1280,80]{2,3,1,0:T(8,128)(2,1)}, u32[]{:S(2)}) copy-start(bf16[3,3,1280,80]{2,3,1,0:T(8,128)(2,1)} %param.20) | copy-start | bytes 5529604
  154.3 11.6 %slice-start.6 = ((s8[5898240]{0:T(1024)(128)(4,1)}), s8[4194304]{0:T(1024)(128)(4,1)S(1)}, s32[]{:S(2)}) async-start(s8[5898240]{0:T(1024)(128)(4,1)} %bitcast.125), calls=%async_computation.14 | async-start | bytes 8388608
  159.1 4.8 %copy-start.2 = (bf16[1,1,32,72,1280]{4,3,1,0,2:T(8,128)(2,1)S(1)}, bf16[1,1,32,72,1280]{4,3,1,0,2:T(8,128)(2,1)}, u32[]{:S(2)}) copy-start(bf16[1,1,32,72,1280]{4,3,1,0,2:T(8,128)(2,1)} %get-tuple-element.11) | copy-start | bytes 17694724
  159.1 6.8 %slice-start.7 = ((s8[5898240]{0:T(1024)(128)(4,1)}), s8[1703936]{0:T(1024)(128)(4,1)S(1)}, s32[]{:S(2)}) async-start(s8[5898240]{0:T(1024)(128)(4,1)} %bitcast.125), calls=%async_computation.15 | async-start | bytes 3407872
  163.9 3.9 slice-start
  163.9 6.1 %slice-start.4 = ((s8[5898240]{0:T(1024)(128)(4,1)}), s8[4194304]{0:T(1024)(128)(4,1)S(1)}, s32[]{:S(2)}) async-start(s8[5898240]{0:T(1024)(128)(4,1)} %bitcast.122), calls=%async_computation.12 | async-start | bytes 8388608
  165.9 2.2 slice-start.1
  165.9 4.1 %slice-start.5 = ((s8[5898240]{0:T(1024)(128)(4,1)}), s8[1703936]{0:T(1024)(128)(4,1)S(1)}, s32[]{:S(2)}) async-start(s8[5898240]{0:T(1024)(128)(4,1)} %bitcast.122), calls=%async_computation.13 | async-start | bytes 3407872
  168.1 3.9 slice-start.2
  170.1 2.2 slice-start.3
  179.0 25.0 %copy-start.7 = (f32[1280]{0:T(1024)S(1)}, f32[1280]{0:T(1024)}, u32[]{:S(2)}) copy-start(f32[1280]{0:T(1024)} %param.21) | copy-start | bytes 15364
  179.0 25.5 %copy-start.8 = (f32[1280]{0:T(1024)S(1)}, f32[1280]{0:T(1024)}, u32[]{:S(2)}) copy-start(f32[1280]{0:T(1024)} %param.22) | copy-start | bytes 15364
  289.1 29.5 %all-to-all-start.2 = ((bf16[1,16,9,1280]{3,2,0,1:T(8,128)(2,1)}), bf16[1,16,9,1280]{3,2,0,1:T(8,128)(2,1)S(1)}, u32[]{:S(2)}, u32[]{:S(2)}) async-start(bf16[1,16,9,1280]{3,2,0,1:T(8,128)(2,1)} %bitcast.32), calls=%async_computation.2 | async-start | bytes 1310720 | tf_op jit(solution)/shard_map/all_to_all | solution.py:124
  296.7 49.4 %copy-start.9 = (f32[20]{0:T(128)S(1)}, f32[20]{0:T(128)}, u32[]{:S(2)}) copy-start(f32[20]{0:T(128)} %param.25) | copy-start | bytes 244
  318.6 23.9 %all-to-all-start.3 = ((bf16[1,16,9,1280]{3,2,0,1:T(8,128)(2,1)}), bf16[1,16,9,1280]{3,2,0,1:T(8,128)(2,1)S(1)}, u32[]{:S(2)}, u32[]{:S(2)}) async-start(bf16[1,16,9,1280]{3,2,0,1:T(8,128)(2,1)} %bitcast.34), calls=%async_computation.3 | async-start | bytes 1310720 | tf_op jit(solution)/shard_map/all_to_all | solution.py:125
  342.5 25.0 %all-to-all-start.1 = ((bf16[1,16,9,1280]{3,2,0,1:T(8,128)(2,1)}), bf16[1,16,9,1280]{3,2,0,1:T(8,128)(2,1)S(1)}, u32[]{:S(2)}, u32[]{:S(2)}) async-start(bf16[1,16,9,1280]{3,2,0,1:T(8,128)(2,1)} %bitcast.30), calls=%async_computation.1 | async-start | bytes 1310720 | tf_op jit(solution)/shard_map/all_to_all | solution.py:126
  372.3 33.0 %copy-start.1 = (bf16[64,2560]{1,0:T(8,128)(2,1)S(1)}, bf16[64,2560]{1,0:T(8,128)(2,1)}, u32[]{:S(2)}) copy-start(bf16[64,2560]{1,0:T(8,128)(2,1)} %param.18) | copy-start | bytes 983044
Sparse Core Ops, SparseCore 0:
  68.6 50.0 all-gather.4
  121.3 163.6 all-gather.6
  287.5 112.4 all-gather.8
